TPU v7x, 32 devices: a whole 2x2x4 slice. The times are simulated.
32 devices in a mesh: req: 8 (over y, x, core), head: 4 (over z).
Axes of the slice: x: 2, y: 2, z: 4, core: 2. Of those that a mesh axis runs over, the one named last changes fastest.
Arguments:
- queries: bfloat16 [4096, 8192], P('req', 'head'), may hold values from -150 to 150, as said below
- new_keys: bfloat16 [4096, 1024], P('req', 'head'), may hold values from -6 to 6, as said below
- fresh_values: bfloat16 [4096, 1024], P('req', 'head'), may hold values from -6 to 6
- key_page_pool: bfloat16 [224, 128, 1024], P('req', None, 'head'), may hold values from -6 to 6
- value_page_pool: bfloat16 [224, 128, 1024], P('req', None, 'head'), may hold values from -6 to 6
- page_table: int32 [16, 14], P('req'), may hold values from 0 to 27, as said below
- new_counts: int32 [16], P('req'), may hold values from 1 to 256, 2048 in all
- cached_lens: int32 [16], P('req'), may hold values from 1 to 1536, 8192 in all
- deal_offset: int32 [8], P('req'), may hold values from 0 to 7
- residual: bfloat16 [2112, 8192], P('req', 'head'), may hold values from -1.1953125 to 1.1953125
- out_weight: bfloat16 [8192, 8192], P('head', 'req'), may hold values from -0.09375 to 0.09375
Outputs:
- hidden: bfloat16 [2112, 8192], P('req', 'head')
- keys_out: bfloat16 [224, 128, 1024], P('req', None, 'head')
- values_out: bfloat16 [224, 128, 1024], P('req', None, 'head')
Inputs may be any that keep to these rules, and one draw needn't show every extreme that they name: `new_counts`: the counts sum to 2048; the largest is exactly 256. `cached_lens`: the counts sum to 8192; the largest is exactly 1536. `page_table`: the 2 rows of each aligned block of requests hold together each of 0 to 27 once. `queries`: real values. `new_keys`: real values.
All inputs are finite; a program needn't handle non-finite values. No bound on the sum of `new_counts` or of `cached_lens` on one device may be relied on, other than what follows from the above.
Results may differ from a plain program's by a relative error of at most 0.0085.
Values may be sent and summed in bfloat16 or wider, within the bound.
No kernel may reach another device: no remote copies, remote signals or barrier semaphores. Data moves between devices by JAX's collectives and lax.ppermute only.
A program may use at most 128 MiB of HBM per device.

v0:
```python
import math
import jax
import jax.numpy as jnp
from jax import lax
from jax.sharding import PartitionSpec as P

HEAD_SIZE = 128
NEGATIVE = -1e30


def head_attention(query_matrix, prior_keys, prior_values, visible, scale_factor):
    scores = (
        jnp.einsum("tkd,skd->kts", query_matrix, prior_keys, preferred_element_type=jnp.float32)
        * scale_factor
    )
    spots_all = jnp.arange(prior_keys.shape[0], dtype=jnp.int32)
    allowed = spots_all[None, None, :] <= visible[None, :, None]
    scores = jnp.where(allowed, scores, NEGATIVE)
    highest = jnp.max(scores, axis=2, keepdims=True)
    expo_terms = jnp.where(allowed, jnp.exp(scores - highest), 0.0)
    weights = (expo_terms / jnp.sum(expo_terms, axis=2, keepdims=True)).astype(jnp.bfloat16)
    mixed = jnp.einsum("kts,skd->tkd", weights, prior_values, preferred_element_type=jnp.float32)
    return mixed.astype(jnp.bfloat16)


def deal(row_block, new_counts, lead_in, shares, starts, totals, balanced):
    groups = lax.axis_size("req")
    my_rank = lax.axis_index("req")
    per_group = new_counts.shape[0]
    new_limit = row_block.shape[0] // per_group
    pair_slots = row_block.shape[0] // groups
    columns = row_block.shape[1]
    own_lead = lax.dynamic_index_in_dim(lead_in, my_rank, 0, keepdims=False)
    ordinal = jnp.arange(pair_slots, dtype=jnp.int32)[None, :] * groups + own_lead[:, None]
    ends_at = jnp.cumsum(new_counts)
    request_index = jnp.sum(
        (ordinal[:, :, None] >= ends_at[None, None, :]).astype(jnp.int32), axis=2
    )
    request_index = jnp.minimum(request_index, per_group - 1)
    before = ends_at - new_counts
    source = request_index * new_limit + ordinal - jnp.take(before, request_index)
    own_total = lax.dynamic_index_in_dim(totals, my_rank, 0, keepdims=False)
    is_live = ordinal < own_total
    source = jnp.where(is_live, source, 0)
    picked = jnp.take(row_block, source.reshape(-1), axis=0).reshape(groups, pair_slots, columns)
    outgoing = jnp.where(is_live[:, :, None], picked, jnp.zeros((), row_block.dtype))
    arrived = lax.all_to_all(outgoing, "req", split_axis=0, concat_axis=0, tiled=True)
    own_shares = lax.dynamic_index_in_dim(shares, my_rank, 1, keepdims=False)
    own_starts = lax.dynamic_index_in_dim(starts, my_rank, 1, keepdims=False)
    within = jnp.arange(pair_slots, dtype=jnp.int32)[None, :]
    landing = jnp.where(within < own_shares[:, None], own_starts[:, None] + within, balanced)
    blank_rows = jnp.zeros((balanced, columns), row_block.dtype)
    return blank_rows.at[landing.reshape(-1)].set(arrived.reshape(-1, columns), mode="drop")


def project(row_block, out_weight):
    return jnp.dot(
        row_block,
        lax.all_gather(out_weight, "req", axis=1, tiled=True),
        preferred_element_type=jnp.float32,
    )


def head_total(partial_sum):
    return lax.psum_scatter(
        partial_sum.astype(jnp.bfloat16), "head", scatter_dimension=1, tiled=True
    ).astype(jnp.float32)


def local(
    queries,
    new_keys,
    fresh_values,
    key_page_pool,
    value_page_pool,
    page_table,
    new_counts,
    cached_lens,
    deal_offset,
    residual,
    out_weight,
):
    groups = lax.axis_size("req")
    per_group = new_counts.shape[0]
    page_count = page_table.shape[1]
    page_rows = key_page_pool.shape[1]
    channel_count = key_page_pool.shape[2]
    kv_local = channel_count // HEAD_SIZE
    slot_count = queries.shape[0]
    new_limit = slot_count // per_group
    q_width = queries.shape[1]
    group_fanout = q_width // channel_count
    balanced = residual.shape[0]
    new_slot = jnp.arange(new_limit, dtype=jnp.int32)
    positions = cached_lens[:, None] + new_slot[None, :]
    page_of = jnp.take_along_axis(page_table, positions // page_rows, axis=1)
    outside = key_page_pool.shape[0] * page_rows
    target = jnp.where(
        new_slot[None, :] < new_counts[:, None],
        page_of * page_rows + positions % page_rows,
        outside,
    ).reshape(-1)
    flat_keys = key_page_pool.reshape(-1, channel_count).at[target].set(new_keys, mode="drop")
    flat_values = (
        value_page_pool.reshape(-1, channel_count).at[target].set(fresh_values, mode="drop")
    )
    gathered_keys = flat_keys.reshape(key_page_pool.shape)
    gathered_values = flat_values.reshape(value_page_pool.shape)
    scale_factor = 1.0 / math.sqrt(HEAD_SIZE)
    pieces = []
    for member in range(per_group):
        prior_keys = gathered_keys[page_table[member]].reshape(
            page_count * page_rows, kv_local, HEAD_SIZE
        )
        prior_values = gathered_values[page_table[member]].reshape(
            page_count * page_rows, kv_local, HEAD_SIZE
        )
        query_matrix = queries[member * new_limit : (member + 1) * new_limit].reshape(
            new_limit, kv_local, group_fanout, HEAD_SIZE
        )
        query_matrix = jnp.moveaxis(query_matrix, 2, 0)
        visible = positions[member]
        mixed = lax.map(
            lambda single: head_attention(single, prior_keys, prior_values, visible, scale_factor),
            query_matrix,
        )
        pieces.append(jnp.moveaxis(mixed, 0, 2).reshape(new_limit, q_width))
    attended = jnp.concatenate(pieces, axis=0)
    load_counts, offsets_all = (
        lax.all_gather(new_counts, "req", axis=0, tiled=True),
        lax.all_gather(deal_offset, "req", axis=0, tiled=True),
    )
    totals = jnp.sum(load_counts.reshape(groups, per_group), axis=1)
    rank_ids = jnp.arange(groups, dtype=jnp.int32)
    lead_in = jnp.remainder(rank_ids[None, :] - offsets_all[:, None], groups)
    shares = jnp.maximum((totals[:, None] - lead_in + groups - 1) // groups, 0)
    starts = jnp.cumsum(shares, axis=0) - shares
    summed = head_total(project(attended, out_weight)).astype(jnp.bfloat16)
    placed = deal(summed, new_counts, lead_in, shares, starts, totals, balanced)
    hidden = (residual.astype(jnp.float32) + placed.astype(jnp.float32)).astype(jnp.bfloat16)
    return (hidden, gathered_keys, gathered_values)


def solution(mesh):
    placed = (
        P("req", "head"),
        P("req", "head"),
        P("req", "head"),
        P("req", None, "head"),
        P("req", None, "head"),
        P("req", None),
        P("req"),
        P("req"),
        P("req"),
        P("req", "head"),
        P("head", "req"),
    )
    return jax.shard_map(
        local,
        mesh=mesh,
        in_specs=placed,
        out_specs=(P("req", "head"), P("req", None, "head"), P("req", None, "head")),
        check_vma=False,
    )
```

profile of v0, /device:TPU:0, one launch (start us, length us, event | category | flops | bytes accessed | tf_op | source)
XLA Modules:
  0.0 404.9 jit_solution(16835856660951470666)
XLA Ops:
  7.2 2.9 copy.77
  11.1 4.7 %gather_fusion.6 = s32[512]{0:T(512)S(1)} fusion(s32[2,14]{1,0:T(2,128)S(1)} %copy-done, s32[512]{0:T(512)S(1)} %bitcast.125), kind=kCustom, calls=%fused_computation.6 | custom fusion | bytes 8192 | tf_op jit(solution)/shard_map/jit(take_along_axis)/gather | solution.py:96
  15.9 5.5 %scatter_fusion = bf16[3584,256]{1,0:T(8,128)(2,1)} fusion(bf16[3584,256]{1,0:T(8,128)(2,1)} %bitcast.130, s32[512]{0:T(512)S(1)} %bitcast.143, bf16[512,256]{1,0:T(8,128)(2,1)S(1)} %copy-done.7), kind=kCustom, calls=%fused_computation.7 | custom fusion | bytes 788480 | tf_op jit(solution)/shard_map/scatter | solution.py:103
  21.4 3.5 gather_fusion.3
  25.0 3.6 scatter_fusion.1
  30.1 3.1 gather_fusion.1
  48.2 66.8 %while.21 = (s32[]{:T(128)}, bf16[8,256,2,128]{1,3,0,2:T(8,128)(2,1)S(1)}, s32[1,256]{1,0:T(1,128)S(1)}, bf16[8,256,2,128]{1,3,0,2:T(8,128)(2,1)}, bf16[1792,2,1...) while((s32[]{:T(128)}, bf16[8,256,2,128]{1,3,0,2:T(8,128)(2,1)S(1)}, ...), condition=%wide.region_13.14_spmd, body=%wide.region_10.13_spmd.sunk | while | flops 476710656 | bytes 11342941 | solution.py:123
  48.5 4.6 %fusion.93 = (f32[2,256]{1,0:T(2,128)S(1)}, f32[2,256,1792]{2,1,0:T(8,128)}) fusion(bf16[1792,2,128]{2,0,1:T(8,128)(2,1)S(1)} %get-tuple-element.251, pred[256,1792]{1,0:T(8,128)(4,1)S(1)} %iota_compare_fusion.6, bf16[8,256,2,128]{1,3,0,2:T(8,128)(2,1)} %get-tuple-element.250, s32[]{:T(128)S(6)} %copy.63), kind=kOutput, calls=%fused_computation.132.clone.1 | convolution fusion | flops 239470336 | bytes 5638148 | tf_op jit(solution)/shard_map/while/body/eval_jaxpr/sub | solution.py:20
  53.1 3.0 fusion.94
  56.6 4.6 %fusion.93 = (f32[2,256]{1,0:T(2,128)S(1)}, f32[2,256,1792]{2,1,0:T(8,128)}) fusion(bf16[1792,2,128]{2,0,1:T(8,128)(2,1)S(1)} %get-tuple-element.251, pred[256,1792]{1,0:T(8,128)(4,1)S(1)} %iota_compare_fusion.6, bf16[8,256,2,128]{1,3,0,2:T(8,128)(2,1)} %get-tuple-element.250, s32[]{:T(128)S(6)} %copy.63), kind=kOutput, calls=%fused_computation.132.clone.1 | convolution fusion | flops 239470336 | bytes 5638148 | tf_op jit(solution)/shard_map/while/body/eval_jaxpr/sub | solution.py:20
  61.3 3.0 fusion.94
  64.7 4.6 %fusion.93 = (f32[2,256]{1,0:T(2,128)S(1)}, f32[2,256,1792]{2,1,0:T(8,128)}) fusion(bf16[1792,2,128]{2,0,1:T(8,128)(2,1)S(1)} %get-tuple-element.251, pred[256,1792]{1,0:T(8,128)(4,1)S(1)} %iota_compare_fusion.6, bf16[8,256,2,128]{1,3,0,2:T(8,128)(2,1)} %get-tuple-element.250, s32[]{:T(128)S(6)} %copy.63), kind=kOutput, calls=%fused_computation.132.clone.1 | convolution fusion | flops 239470336 | bytes 5638148 | tf_op jit(solution)/shard_map/while/body/eval_jaxpr/sub | solution.py:20
  69.4 3.0 fusion.94
  72.8 4.6 %fusion.93 = (f32[2,256]{1,0:T(2,128)S(1)}, f32[2,256,1792]{2,1,0:T(8,128)}) fusion(bf16[1792,2,128]{2,0,1:T(8,128)(2,1)S(1)} %get-tuple-element.251, pred[256,1792]{1,0:T(8,128)(4,1)S(1)} %iota_compare_fusion.6, bf16[8,256,2,128]{1,3,0,2:T(8,128)(2,1)} %get-tuple-element.250, s32[]{:T(128)S(6)} %copy.63), kind=kOutput, calls=%fused_computation.132.clone.1 | convolution fusion | flops 239470336 | bytes 5638148 | tf_op jit(solution)/shard_map/while/body/eval_jaxpr/sub | solution.py:20
  77.5 4.4 %fusion.94 = bf16[1,256,2,128]{3,1,2,0:T(8,128)(2,1)S(1)} fusion(bf16[1792,2,128]{2,0,1:T(8,128)(2,1)} %get-tuple-element.252, f32[2,256,1792]{2,1,0:T(8,128)} %get-tuple-element.231, f32[2,256]{1,0:T(2,128)S(1)} %get-tuple-element.232), kind=kOutput, calls=%fused_computation.37.clone.1 | convolution fusion | flops 236781568 | bytes 4720640 | tf_op jit(solution)/shard_map/while/body/eval_jaxpr/kts,skd->tkd/dot_general | solution.py:22
  82.3 4.7 %fusion.93 = (f32[2,256]{1,0:T(2,128)S(1)}, f32[2,256,1792]{2,1,0:T(8,128)}) fusion(bf16[1792,2,128]{2,0,1:T(8,128)(2,1)S(1)} %get-tuple-element.251, pred[256,1792]{1,0:T(8,128)(4,1)S(1)} %iota_compare_fusion.6, bf16[8,256,2,128]{1,3,0,2:T(8,128)(2,1)} %get-tuple-element.250, s32[]{:T(128)S(6)} %copy.63), kind=kOutput, calls=%fused_computation.132.clone.1 | convolution fusion | flops 239470336 | bytes 5638148 | tf_op jit(solution)/shard_map/while/body/eval_jaxpr/sub | solution.py:20
  87.0 3.0 fusion.94
  90.5 4.6 %fusion.93 = (f32[2,256]{1,0:T(2,128)S(1)}, f32[2,256,1792]{2,1,0:T(8,128)}) fusion(bf16[1792,2,128]{2,0,1:T(8,128)(2,1)S(1)} %get-tuple-element.251, pred[256,1792]{1,0:T(8,128)(4,1)S(1)} %iota_compare_fusion.6, bf16[8,256,2,128]{1,3,0,2:T(8,128)(2,1)} %get-tuple-element.250, s32[]{:T(128)S(6)} %copy.63), kind=kOutput, calls=%fused_computation.132.clone.1 | convolution fusion | flops 239470336 | bytes 5638148 | tf_op jit(solution)/shard_map/while/body/eval_jaxpr/sub | solution.py:20
  95.1 3.0 fusion.94
  98.6 4.6 %fusion.93 = (f32[2,256]{1,0:T(2,128)S(1)}, f32[2,256,1792]{2,1,0:T(8,128)}) fusion(bf16[1792,2,128]{2,0,1:T(8,128)(2,1)S(1)} %get-tuple-element.251, pred[256,1792]{1,0:T(8,128)(4,1)S(1)} %iota_compare_fusion.6, bf16[8,256,2,128]{1,3,0,2:T(8,128)(2,1)} %get-tuple-element.250, s32[]{:T(128)S(6)} %copy.63), kind=kOutput, calls=%fused_computation.132.clone.1 | convolution fusion | flops 239470336 | bytes 5638148 | tf_op jit(solution)/shard_map/while/body/eval_jaxpr/sub | solution.py:20
  103.2 3.5 fusion.94
  107.2 4.6 %fusion.93 = (f32[2,256]{1,0:T(2,128)S(1)}, f32[2,256,1792]{2,1,0:T(8,128)}) fusion(bf16[1792,2,128]{2,0,1:T(8,128)(2,1)S(1)} %get-tuple-element.251, pred[256,1792]{1,0:T(8,128)(4,1)S(1)} %iota_compare_fusion.6, bf16[8,256,2,128]{1,3,0,2:T(8,128)(2,1)} %get-tuple-element.250, s32[]{:T(128)S(6)} %copy.63), kind=kOutput, calls=%fused_computation.132.clone.1 | convolution fusion | flops 239470336 | bytes 5638148 | tf_op jit(solution)/shard_map/while/body/eval_jaxpr/sub | solution.py:20
  111.9 3.0 fusion.94
  115.1 65.1 %while.20 = (s32[]{:T(128)}, bf16[8,256,2,128]{1,3,0,2:T(8,128)(2,1)S(1)}, s32[1,256]{1,0:T(1,128)S(1)}, bf16[8,256,2,128]{1,3,0,2:T(8,128)(2,1)}, bf16[1792,2,1...) while((s32[]{:T(128)}, bf16[8,256,2,128]{1,3,0,2:T(8,128)(2,1)S(1)}, ...), condition=%wide.region_9.10_spmd, body=%wide.region_6.9_spmd.sunk | while | flops 476710656 | bytes 11342941 | solution.py:123
  115.5 4.6 %fusion.88 = (f32[2,256]{1,0:T(2,128)S(1)}, f32[2,256,1792]{2,1,0:T(8,128)}) fusion(bf16[1792,2,128]{2,0,1:T(8,128)(2,1)S(1)} %get-tuple-element.272, pred[256,1792]{1,0:T(8,128)(4,1)S(1)} %iota_compare_fusion.5, bf16[8,256,2,128]{1,3,0,2:T(8,128)(2,1)} %get-tuple-element.271, s32[]{:T(128)S(6)} %copy.69), kind=kOutput, calls=%fused_computation.131.clone.1 | convolution fusion | flops 239470336 | bytes 5638148 | tf_op jit(solution)/shard_map/while/body/eval_jaxpr/sub | solution.py:20
  120.1 3.0 fusion.89
  123.6 4.6 %fusion.88 = (f32[2,256]{1,0:T(2,128)S(1)}, f32[2,256,1792]{2,1,0:T(8,128)}) fusion(bf16[1792,2,128]{2,0,1:T(8,128)(2,1)S(1)} %get-tuple-element.272, pred[256,1792]{1,0:T(8,128)(4,1)S(1)} %iota_compare_fusion.5, bf16[8,256,2,128]{1,3,0,2:T(8,128)(2,1)} %get-tuple-element.271, s32[]{:T(128)S(6)} %copy.69), kind=kOutput, calls=%fused_computation.131.clone.1 | convolution fusion | flops 239470336 | bytes 5638148 | tf_op jit(solution)/shard_map/while/body/eval_jaxpr/sub | solution.py:20
  128.2 3.0 fusion.89
  131.7 4.6 %fusion.88 = (f32[2,256]{1,0:T(2,128)S(1)}, f32[2,256,1792]{2,1,0:T(8,128)}) fusion(bf16[1792,2,128]{2,0,1:T(8,128)(2,1)S(1)} %get-tuple-element.272, pred[256,1792]{1,0:T(8,128)(4,1)S(1)} %iota_compare_fusion.5, bf16[8,256,2,128]{1,3,0,2:T(8,128)(2,1)} %get-tuple-element.271, s32[]{:T(128)S(6)} %copy.69), kind=kOutput, calls=%fused_computation.131.clone.1 | convolution fusion | flops 239470336 | bytes 5638148 | tf_op jit(solution)/shard_map/while/body/eval_jaxpr/sub | solution.py:20
  136.3 3.2 fusion.89
  140.0 4.6 %fusion.88 = (f32[2,256]{1,0:T(2,128)S(1)}, f32[2,256,1792]{2,1,0:T(8,128)}) fusion(bf16[1792,2,128]{2,0,1:T(8,128)(2,1)S(1)} %get-tuple-element.272, pred[256,1792]{1,0:T(8,128)(4,1)S(1)} %iota_compare_fusion.5, bf16[8,256,2,128]{1,3,0,2:T(8,128)(2,1)} %get-tuple-element.271, s32[]{:T(128)S(6)} %copy.69), kind=kOutput, calls=%fused_computation.131.clone.1 | convolution fusion | flops 239470336 | bytes 5638148 | tf_op jit(solution)/shard_map/while/body/eval_jaxpr/sub | solution.py:20
  144.6 3.0 fusion.89
  148.1 4.6 %fusion.88 = (f32[2,256]{1,0:T(2,128)S(1)}, f32[2,256,1792]{2,1,0:T(8,128)}) fusion(bf16[1792,2,128]{2,0,1:T(8,128)(2,1)S(1)} %get-tuple-element.272, pred[256,1792]{1,0:T(8,128)(4,1)S(1)} %iota_compare_fusion.5, bf16[8,256,2,128]{1,3,0,2:T(8,128)(2,1)} %get-tuple-element.271, s32[]{:T(128)S(6)} %copy.69), kind=kOutput, calls=%fused_computation.131.clone.1 | convolution fusion | flops 239470336 | bytes 5638148 | tf_op jit(solution)/shard_map/while/body/eval_jaxpr/sub | solution.py:20
  152.7 3.0 fusion.89
  156.2 4.6 %fusion.88 = (f32[2,256]{1,0:T(2,128)S(1)}, f32[2,256,1792]{2,1,0:T(8,128)}) fusion(bf16[1792,2,128]{2,0,1:T(8,128)(2,1)S(1)} %get-tuple-element.272, pred[256,1792]{1,0:T(8,128)(4,1)S(1)} %iota_compare_fusion.5, bf16[8,256,2,128]{1,3,0,2:T(8,128)(2,1)} %get-tuple-element.271, s32[]{:T(128)S(6)} %copy.69), kind=kOutput, calls=%fused_computation.131.clone.1 | convolution fusion | flops 239470336 | bytes 5638148 | tf_op jit(solution)/shard_map/while/body/eval_jaxpr/sub | solution.py:20
  160.8 3.0 fusion.89
  164.3 4.6 %fusion.88 = (f32[2,256]{1,0:T(2,128)S(1)}, f32[2,256,1792]{2,1,0:T(8,128)}) fusion(bf16[1792,2,128]{2,0,1:T(8,128)(2,1)S(1)} %get-tuple-element.272, pred[256,1792]{1,0:T(8,128)(4,1)S(1)} %iota_compare_fusion.5, bf16[8,256,2,128]{1,3,0,2:T(8,128)(2,1)} %get-tuple-element.271, s32[]{:T(128)S(6)} %copy.69), kind=kOutput, calls=%fused_computation.131.clone.1 | convolution fusion | flops 239470336 | bytes 5638148 | tf_op jit(solution)/shard_map/while/body/eval_jaxpr/sub | solution.py:20
  168.9 3.0 fusion.89
  172.4 4.6 %fusion.88 = (f32[2,256]{1,0:T(2,128)S(1)}, f32[2,256,1792]{2,1,0:T(8,128)}) fusion(bf16[1792,2,128]{2,0,1:T(8,128)(2,1)S(1)} %get-tuple-element.272, pred[256,1792]{1,0:T(8,128)(4,1)S(1)} %iota_compare_fusion.5, bf16[8,256,2,128]{1,3,0,2:T(8,128)(2,1)} %get-tuple-element.271, s32[]{:T(128)S(6)} %copy.69), kind=kOutput, calls=%fused_computation.131.clone.1 | convolution fusion | flops 239470336 | bytes 5638148 | tf_op jit(solution)/shard_map/while/body/eval_jaxpr/sub | solution.py:20
  177.0 3.0 fusion.89
  180.2 25.9 %convolution_convert_fusion = bf16[512,8192]{1,0:T(8,128)(2,1)} fusion(bf16[2048,8192]{1,0:T(8,128)(2,1)} %all-gather.2.cloned.1.call-done, bf16[256,2048]{0,1:T(8,128)(2,1)S(1)} %bitcast.138, bf16[256,2048]{0,1:T(8,128)(2,1)S(1)} %bitcast.139), kind=kOutput, calls=%fused_computation.48 | convolution fusion | flops 17188257792 | bytes 44040192 | tf_op jit(solution)/shard_map/dot_general | solution.py:57
  209.1 9.2 %all-reduce.2 = (s32[16]{0:T(128)S(1)}, s32[8]{0:T(128)S(1)}) all-reduce(s32[16]{0:T(128)S(1)} %dynamic-update-slice, s32[8]{0:T(128)S(1)} %dynamic-update-slice.1), channel_id=1, replica_groups=mesh['req'=8,'head'=4] {'req'}, use_global_device_ids=true, to_apply=%add | all-reduce | flops 24 | bytes 192
  219.8 3.6 gather_fusion
  224.9 128.4 %reduce-scatter.2.cloned.1.call-done = bf16[512,2048]{1,0:T(8,128)(2,1)} async-done(((bf16[512,8192]{1,0:T(8,128)(2,1)}), bf16[512,2048]{1,0:T(8,128)(2,1)}) %reduce-scatter.2.cloned.1.call-update) | async-done | bytes 2097168 | tf_op jit(solution)/shard_map/reduce_scatter | solution.py:65
  353.4 6.3 %gather_fusion.5 = bf16[512,2048]{1,0:T(8,128)(2,1)S(1)} fusion(bf16[512,2048]{1,0:T(8,128)(2,1)} %reduce-scatter.2.cloned.1.call-done, s32[1024]{0:T(1024)S(1)} %pad_clamp_fusion), kind=kCustom, calls=%fused_computation.5 | custom fusion | bytes 4196352 | tf_op jit(solution)/shard_map/jit(_take)/gather | solution.py:45
  361.4 3.6 all-to-all-start
  365.4 26.2 %all-to-all-done = bf16[8,64,2048]{2,1,0:T(8,128)(2,1)S(1)} async-done(((bf16[8,64,2048]{2,1,0:T(8,128)(2,1)}), bf16[8,64,2048]{2,1,0:T(8,128)(2,1)S(1)}, u32[]{:S(2)}, u32[]{:S(2)}) %all-to-all-start) | async-done | bytes 2097184 | tf_op jit(solution)/shard_map/all_to_all | solution.py:47
  391.6 3.8 scatter_custom_fusion.2
  (139 shorter events, 34.2 us)
Async XLA Ops:
  7.2 173.0 %all-gather.2.cloned.1.call-start = ((), (), s32[]{:S(2)}) async-start(), calls=%async_computation.2 | async-start | bytes 37748736 | tf_op jit(solution)/shard_map/all_gather | solution.py:59
  10.1 0.7 copy-start.9
  10.1 0.9 copy-start.10
  10.1 0.9 copy-start
  10.2 5.7 %copy-start.7 = (bf16[512,256]{1,0:T(8,128)(2,1)S(1)}, bf16[512,256]{1,0:T(8,128)(2,1)}, u32[]{:S(2)}) copy-start(bf16[512,256]{1,0:T(8,128)(2,1)} %param.16) | copy-start | bytes 786436
  10.2 343.2 %reduce-scatter.2.cloned.1.call-start = ((), (), s32[]{:S(2)}) async-start(), calls=%async_computation.3 | async-start | bytes 10485760 | tf_op jit(solution)/shard_map/reduce_scatter | solution.py:65
  15.9 9.1 %copy-start.2 = (bf16[28,128,256]{2,1,0:T(8,128)(2,1)S(1)}, bf16[28,128,256]{2,1,0:T(8,128)(2,1)}, u32[]{:S(2)}) copy-start(bf16[28,128,256]{2,1,0:T(8,128)(2,1)} %param.19) | copy-start | bytes 5505028
  15.9 9.1 %copy-start.8 = (bf16[512,256]{1,0:T(8,128)(2,1)S(1)}, bf16[512,256]{1,0:T(8,128)(2,1)}, u32[]{:S(2)}) copy-start(bf16[512,256]{1,0:T(8,128)(2,1)} %param.17) | copy-start | bytes 786436
  28.5 6.2 %copy-start.1 = (bf16[3584,256]{1,0:T(8,128)(2,1)}, bf16[3584,256]{1,0:T(8,128)(2,1)S(1)}, u32[]{:S(2)}) copy-start(bf16[3584,256]{1,0:T(8,128)(2,1)S(1)} %scatter_fusion.1) | copy-start | bytes 5505028
  37.4 2.4 copy-start.4
  40.0 1.5 copy-start.5
  44.1 2.4 copy-start.3
  46.7 1.5 copy-start.6
  206.1 0.7 copy-start.11
  361.4 30.3 %all-to-all-start = ((bf16[8,64,2048]{2,1,0:T(8,128)(2,1)}), bf16[8,64,2048]{2,1,0:T(8,128)(2,1)S(1)}, u32[]{:S(2)}, u32[]{:S(2)}) async-start(bf16[8,64,2048]{2,1,0:T(8,128)(2,1)} %select_select_fusion), calls=%async_computation.1 | async-start | bytes 4194304 | tf_op jit(solution)/shard_map/all_to_all | solution.py:47
Sparse Core Ops, SparseCore 0:
  10.3 163.3 all-gather.1
  206.3 147.0 reduce-scatter.1
where the time goes:
time: 406 us; the launch traced here: 405 us
  waiting for transfers between devices  155 us (38%)
  matrix products  150 us (37%)
  local copies, waits for them, and re-layouts  59.2 us (15%)
  between operations  15.6 us (4%)
  other arithmetic  11.8 us (3%)
  blocking collectives  9.17 us (2%)
    reduce_scatter x1, waiting for transfers between devices, head_total(): lax.psum_scatter(partial_sum.astype(jnp.bfloat16), 'head', scatter_dimens...  128 us
    sub x16, matrix products, head_attention(): expo_terms = jnp.where(allowed, jnp.exp(scores - highest), 0.0)  74.1 us
    dot_general x16, matrix products, head_attention(): jnp.einsum('kts,skd->tkd', weights, prior_values, preferred_element_type=...  49.8 us
    all_to_all x1, waiting for transfers between devices, deal(): lax.all_to_all(outgoing, 'req', split_axis=0, concat_axis=0, tiled=True)  26.2 us
    dot_general x1, matrix products, project(): jnp.dot(row_block, lax.all_gather(out_weight, 'req', axis=1, tiled=True),...  25.9 us
    unnamed x40, local copies, waits for them, and re-layouts  9.63 us
    unnamed x1, blocking collectives  9.17 us
  transfers between devices with their start and end apart: 3, of which 2 were waited for; matrix products, arithmetic and copies ran while one was open for 44% of the time, Pallas kernels for 0%

commit v1 on v0

--- a/solution.py
+++ b/solution.py
@@ -44,7 +44,19 @@
     source = jnp.where(is_live, source, 0)
     picked = jnp.take(row_block, source.reshape(-1), axis=0).reshape(groups, pair_slots, columns)
     outgoing = jnp.where(is_live[:, :, None], picked, jnp.zeros((), row_block.dtype))
-    arrived = lax.all_to_all(outgoing, "req", split_axis=0, concat_axis=0, tiled=True)
+    ways, here = (lax.axis_size("req"), lax.axis_index("req"))
+    width = outgoing.shape[0] // ways
+    shape = list(outgoing.shape)
+    shape[0] = width
+    height = shape[0]
+    shape[0] = height * ways
+    full = jnp.zeros(shape, outgoing.dtype)
+    for mask in range(ways):
+        part = lax.dynamic_slice_in_dim(outgoing, (here ^ mask) * width, width, axis=0)
+        if mask:
+            part = lax.ppermute(part, "req", [(d, d ^ mask) for d in range(ways)])
+        full = lax.dynamic_update_slice_in_dim(full, part, (here ^ mask) * height, axis=0)
+    arrived = full
     own_shares = lax.dynamic_index_in_dim(shares, my_rank, 1, keepdims=False)
     own_starts = lax.dynamic_index_in_dim(starts, my_rank, 1, keepdims=False)
     within = jnp.arange(pair_slots, dtype=jnp.int32)[None, :]

time: 406 us -> 417 us (1.027)
  waiting for transfers between devices: 155 us -> 162 us
    all_to_all x1 -> x0, waiting for transfers between devices: 26.2 us -> none  [deal(): lax.all_to_all(outgoing, 'req', split_axis=0, concat_axis=0, tiled=True)]
    ppermute x0 -> x7, waiting for transfers between devices: none -> 18.1 us  [deal(): part = lax.ppermute(part, 'req', [(d, d ^ mask) for d in range(ways)])]
    reduce_scatter x1, waiting for transfers between devices: 128 us -> 143 us  [head_total(): lax.psum_scatter(partial_sum.astype(jnp.bfloat16), 'head', scatter_dimens...]
    ppermute x0 -> x7, starting transfers between devices: none -> 7.06 us  [deal(): part = lax.ppermute(part, 'req', [(d, d ^ mask) for d in range(ways)])]
  transfers between devices with their start and end apart: 3 -> 9, of which waited for: 2 -> 5; matrix products, arithmetic and copies ran while one was open for 44% -> 43% of each run, Pallas kernels for 0% -> 0%
where the time goes in v1:
time: 417 us; the launch traced here: 415 us
  waiting for transfers between devices  162 us (39%)
  matrix products  150 us (36%)
  local copies, waits for them, and re-layouts  60.7 us (15%)
  between operations  15.8 us (4%)
  other arithmetic  10.2 us (2%)
  blocking collectives  9.49 us (2%)
  starting transfers between devices  7.13 us (2%)
    reduce_scatter x1, waiting for transfers between devices, head_total(): lax.psum_scatter(partial_sum.astype(jnp.bfloat16), 'head', scatter_dimens...  143 us
    sub x16, matrix products, head_attention(): expo_terms = jnp.where(allowed, jnp.exp(scores - highest), 0.0)  74.2 us
    dot_general x16, matrix products, head_attention(): jnp.einsum('kts,skd->tkd', weights, prior_values, preferred_element_type=...  49.7 us
    dot_general x1, matrix products, project(): jnp.dot(row_block, lax.all_gather(out_weight, 'req', axis=1, tiled=True),...  25.9 us
    ppermute x7, waiting for transfers between devices, deal(): part = lax.ppermute(part, 'req', [(d, d ^ mask) for d in range(ways)])  18.1 us
    unnamed x1, blocking collectives  9.49 us
    unnamed x40, local copies, waits for them, and re-layouts  9.07 us
  transfers between devices with their start and end apart: 9, of which 5 were waited for; matrix products, arithmetic and copies ran while one was open for 43% of the time, Pallas kernels for 0%

profile of v1, /device:TPU:0, one launch (start us, length us, event | category | flops | bytes accessed | tf_op | source)
XLA Modules:
  0.0 415.4 jit_solution(9510954244406747797)
XLA Ops:
  7.2 2.9 copy.85
  13.1 9.5 %all-reduce.2 = (s32[16]{0:T(128)S(1)}, s32[8]{0:T(128)S(1)}) all-reduce(s32[16]{0:T(128)S(1)} %dynamic-update-slice, s32[8]{0:T(128)S(1)} %dynamic-update-slice.1), channel_id=1, replica_groups=mesh['req'=8,'head'=4] {'req'}, use_global_device_ids=true, to_apply=%add | all-reduce | flops 24 | bytes 192
  24.5 3.3 gather_fusion
  27.9 4.8 %gather_fusion.6 = s32[512]{0:T(512)S(1)} fusion(s32[2,14]{1,0:T(2,128)S(1)} %copy-done, s32[512]{0:T(512)S(1)} %bitcast.125), kind=kCustom, calls=%fused_computation.6 | custom fusion | bytes 8192 | tf_op jit(solution)/shard_map/jit(take_along_axis)/gather | solution.py:108
  33.3 5.5 %scatter_fusion = bf16[3584,256]{1,0:T(8,128)(2,1)} fusion(bf16[3584,256]{1,0:T(8,128)(2,1)} %bitcast.130, s32[512]{0:T(512)S(1)} %bitcast.143, bf16[512,256]{1,0:T(8,128)(2,1)S(1)} %copy-done.7), kind=kCustom, calls=%fused_computation.7 | custom fusion | bytes 788480 | tf_op jit(solution)/shard_map/scatter | solution.py:115
  38.8 3.1 gather_fusion.3
  41.9 3.6 scatter_fusion.1
  47.0 3.1 gather_fusion.1
  65.1 66.5 %while.21 = (s32[]{:T(128)}, bf16[8,256,2,128]{1,3,0,2:T(8,128)(2,1)S(1)}, s32[1,256]{1,0:T(1,128)S(1)}, bf16[8,256,2,128]{1,3,0,2:T(8,128)(2,1)}, bf16[1792,2,1...) while((s32[]{:T(128)}, bf16[8,256,2,128]{1,3,0,2:T(8,128)(2,1)S(1)}, ...), condition=%wide.region_13.14_spmd, body=%wide.region_10.13_spmd.sunk | while | flops 476710656 | bytes 11342941 | solution.py:135
  65.4 4.6 %fusion.95 = (f32[2,256]{1,0:T(2,128)S(1)}, f32[2,256,1792]{2,1,0:T(8,128)}) fusion(bf16[1792,2,128]{2,0,1:T(8,128)(2,1)S(1)} %get-tuple-element.259, pred[256,1792]{1,0:T(8,128)(4,1)S(1)} %iota_compare_fusion.6, bf16[8,256,2,128]{1,3,0,2:T(8,128)(2,1)} %get-tuple-element.258, s32[]{:T(128)S(6)} %copy.63), kind=kOutput, calls=%fused_computation.149.clone.1 | convolution fusion | flops 239470336 | bytes 5638148 | tf_op jit(solution)/shard_map/while/body/eval_jaxpr/sub | solution.py:20
  70.0 3.0 fusion.96
  73.5 4.6 %fusion.95 = (f32[2,256]{1,0:T(2,128)S(1)}, f32[2,256,1792]{2,1,0:T(8,128)}) fusion(bf16[1792,2,128]{2,0,1:T(8,128)(2,1)S(1)} %get-tuple-element.259, pred[256,1792]{1,0:T(8,128)(4,1)S(1)} %iota_compare_fusion.6, bf16[8,256,2,128]{1,3,0,2:T(8,128)(2,1)} %get-tuple-element.258, s32[]{:T(128)S(6)} %copy.63), kind=kOutput, calls=%fused_computation.149.clone.1 | convolution fusion | flops 239470336 | bytes 5638148 | tf_op jit(solution)/shard_map/while/body/eval_jaxpr/sub | solution.py:20
  78.1 4.4 %fusion.96 = bf16[1,256,2,128]{3,1,2,0:T(8,128)(2,1)S(1)} fusion(bf16[1792,2,128]{2,0,1:T(8,128)(2,1)} %get-tuple-element.260, f32[2,256,1792]{2,1,0:T(8,128)} %get-tuple-element.239, f32[2,256]{1,0:T(2,128)S(1)} %get-tuple-element.240), kind=kOutput, calls=%fused_computation.37.clone.1 | convolution fusion | flops 236781568 | bytes 4720640 | tf_op jit(solution)/shard_map/while/body/eval_jaxpr/kts,skd->tkd/dot_general | solution.py:22
  83.0 4.7 %fusion.95 = (f32[2,256]{1,0:T(2,128)S(1)}, f32[2,256,1792]{2,1,0:T(8,128)}) fusion(bf16[1792,2,128]{2,0,1:T(8,128)(2,1)S(1)} %get-tuple-element.259, pred[256,1792]{1,0:T(8,128)(4,1)S(1)} %iota_compare_fusion.6, bf16[8,256,2,128]{1,3,0,2:T(8,128)(2,1)} %get-tuple-element.258, s32[]{:T(128)S(6)} %copy.63), kind=kOutput, calls=%fused_computation.149.clone.1 | convolution fusion | flops 239470336 | bytes 5638148 | tf_op jit(solution)/shard_map/while/body/eval_jaxpr/sub | solution.py:20
  87.7 3.0 fusion.96
  91.2 4.6 %fusion.95 = (f32[2,256]{1,0:T(2,128)S(1)}, f32[2,256,1792]{2,1,0:T(8,128)}) fusion(bf16[1792,2,128]{2,0,1:T(8,128)(2,1)S(1)} %get-tuple-element.259, pred[256,1792]{1,0:T(8,128)(4,1)S(1)} %iota_compare_fusion.6, bf16[8,256,2,128]{1,3,0,2:T(8,128)(2,1)} %get-tuple-element.258, s32[]{:T(128)S(6)} %copy.63), kind=kOutput, calls=%fused_computation.149.clone.1 | convolution fusion | flops 239470336 | bytes 5638148 | tf_op jit(solution)/shard_map/while/body/eval_jaxpr/sub | solution.py:20
  95.8 3.0 fusion.96
  99.3 4.6 %fusion.95 = (f32[2,256]{1,0:T(2,128)S(1)}, f32[2,256,1792]{2,1,0:T(8,128)}) fusion(bf16[1792,2,128]{2,0,1:T(8,128)(2,1)S(1)} %get-tuple-element.259, pred[256,1792]{1,0:T(8,128)(4,1)S(1)} %iota_compare_fusion.6, bf16[8,256,2,128]{1,3,0,2:T(8,128)(2,1)} %get-tuple-element.258, s32[]{:T(128)S(6)} %copy.63), kind=kOutput, calls=%fused_computation.149.clone.1 | convolution fusion | flops 239470336 | bytes 5638148 | tf_op jit(solution)/shard_map/while/body/eval_jaxpr/sub | solution.py:20
  103.9 3.1 fusion.96
  107.5 4.6 %fusion.95 = (f32[2,256]{1,0:T(2,128)S(1)}, f32[2,256,1792]{2,1,0:T(8,128)}) fusion(bf16[1792,2,128]{2,0,1:T(8,128)(2,1)S(1)} %get-tuple-element.259, pred[256,1792]{1,0:T(8,128)(4,1)S(1)} %iota_compare_fusion.6, bf16[8,256,2,128]{1,3,0,2:T(8,128)(2,1)} %get-tuple-element.258, s32[]{:T(128)S(6)} %copy.63), kind=kOutput, calls=%fused_computation.149.clone.1 | convolution fusion | flops 239470336 | bytes 5638148 | tf_op jit(solution)/shard_map/while/body/eval_jaxpr/sub | solution.py:20
  112.2 3.0 fusion.96
  115.6 4.6 %fusion.95 = (f32[2,256]{1,0:T(2,128)S(1)}, f32[2,256,1792]{2,1,0:T(8,128)}) fusion(bf16[1792,2,128]{2,0,1:T(8,128)(2,1)S(1)} %get-tuple-element.259, pred[256,1792]{1,0:T(8,128)(4,1)S(1)} %iota_compare_fusion.6, bf16[8,256,2,128]{1,3,0,2:T(8,128)(2,1)} %get-tuple-element.258, s32[]{:T(128)S(6)} %copy.63), kind=kOutput, calls=%fused_computation.149.clone.1 | convolution fusion | flops 239470336 | bytes 5638148 | tf_op jit(solution)/shard_map/while/body/eval_jaxpr/sub | solution.py:20
  120.3 3.0 fusion.96
  123.8 4.6 %fusion.95 = (f32[2,256]{1,0:T(2,128)S(1)}, f32[2,256,1792]{2,1,0:T(8,128)}) fusion(bf16[1792,2,128]{2,0,1:T(8,128)(2,1)S(1)} %get-tuple-element.259, pred[256,1792]{1,0:T(8,128)(4,1)S(1)} %iota_compare_fusion.6, bf16[8,256,2,128]{1,3,0,2:T(8,128)(2,1)} %get-tuple-element.258, s32[]{:T(128)S(6)} %copy.63), kind=kOutput, calls=%fused_computation.149.clone.1 | convolution fusion | flops 239470336 | bytes 5638148 | tf_op jit(solution)/shard_map/while/body/eval_jaxpr/sub | solution.py:20
  128.4 3.0 fusion.96
  131.6 65.3 %while.20 = (s32[]{:T(128)}, bf16[8,256,2,128]{1,3,0,2:T(8,128)(2,1)S(1)}, s32[1,256]{1,0:T(1,128)S(1)}, bf16[8,256,2,128]{1,3,0,2:T(8,128)(2,1)}, bf16[1792,2,1...) while((s32[]{:T(128)}, bf16[8,256,2,128]{1,3,0,2:T(8,128)(2,1)S(1)}, ...), condition=%wide.region_9.10_spmd, body=%wide.region_6.9_spmd.sunk | while | flops 476710656 | bytes 11342941 | solution.py:135
  132.0 4.6 %fusion.90 = (f32[2,256]{1,0:T(2,128)S(1)}, f32[2,256,1792]{2,1,0:T(8,128)}) fusion(bf16[1792,2,128]{2,0,1:T(8,128)(2,1)S(1)} %get-tuple-element.280, pred[256,1792]{1,0:T(8,128)(4,1)S(1)} %iota_compare_fusion.5, bf16[8,256,2,128]{1,3,0,2:T(8,128)(2,1)} %get-tuple-element.279, s32[]{:T(128)S(6)} %copy.69), kind=kOutput, calls=%fused_computation.148.clone.1 | convolution fusion | flops 239470336 | bytes 5638148 | tf_op jit(solution)/shard_map/while/body/eval_jaxpr/sub | solution.py:20
  136.6 3.2 fusion.91
  140.3 4.6 %fusion.90 = (f32[2,256]{1,0:T(2,128)S(1)}, f32[2,256,1792]{2,1,0:T(8,128)}) fusion(bf16[1792,2,128]{2,0,1:T(8,128)(2,1)S(1)} %get-tuple-element.280, pred[256,1792]{1,0:T(8,128)(4,1)S(1)} %iota_compare_fusion.5, bf16[8,256,2,128]{1,3,0,2:T(8,128)(2,1)} %get-tuple-element.279, s32[]{:T(128)S(6)} %copy.69), kind=kOutput, calls=%fused_computation.148.clone.1 | convolution fusion | flops 239470336 | bytes 5638148 | tf_op jit(solution)/shard_map/while/body/eval_jaxpr/sub | solution.py:20
  144.9 3.0 fusion.91
  148.4 4.7 %fusion.90 = (f32[2,256]{1,0:T(2,128)S(1)}, f32[2,256,1792]{2,1,0:T(8,128)}) fusion(bf16[1792,2,128]{2,0,1:T(8,128)(2,1)S(1)} %get-tuple-element.280, pred[256,1792]{1,0:T(8,128)(4,1)S(1)} %iota_compare_fusion.5, bf16[8,256,2,128]{1,3,0,2:T(8,128)(2,1)} %get-tuple-element.279, s32[]{:T(128)S(6)} %copy.69), kind=kOutput, calls=%fused_computation.148.clone.1 | convolution fusion | flops 239470336 | bytes 5638148 | tf_op jit(solution)/shard_map/while/body/eval_jaxpr/sub | solution.py:20
  153.1 3.0 fusion.91
  156.6 4.6 %fusion.90 = (f32[2,256]{1,0:T(2,128)S(1)}, f32[2,256,1792]{2,1,0:T(8,128)}) fusion(bf16[1792,2,128]{2,0,1:T(8,128)(2,1)S(1)} %get-tuple-element.280, pred[256,1792]{1,0:T(8,128)(4,1)S(1)} %iota_compare_fusion.5, bf16[8,256,2,128]{1,3,0,2:T(8,128)(2,1)} %get-tuple-element.279, s32[]{:T(128)S(6)} %copy.69), kind=kOutput, calls=%fused_computation.148.clone.1 | convolution fusion | flops 239470336 | bytes 5638148 | tf_op jit(solution)/shard_map/while/body/eval_jaxpr/sub | solution.py:20
  161.2 3.0 fusion.91
  164.7 4.6 %fusion.90 = (f32[2,256]{1,0:T(2,128)S(1)}, f32[2,256,1792]{2,1,0:T(8,128)}) fusion(bf16[1792,2,128]{2,0,1:T(8,128)(2,1)S(1)} %get-tuple-element.280, pred[256,1792]{1,0:T(8,128)(4,1)S(1)} %iota_compare_fusion.5, bf16[8,256,2,128]{1,3,0,2:T(8,128)(2,1)} %get-tuple-element.279, s32[]{:T(128)S(6)} %copy.69), kind=kOutput, calls=%fused_computation.148.clone.1 | convolution fusion | flops 239470336 | bytes 5638148 | tf_op jit(solution)/shard_map/while/body/eval_jaxpr/sub | solution.py:20
  169.3 3.2 fusion.91
  173.0 4.6 %fusion.90 = (f32[2,256]{1,0:T(2,128)S(1)}, f32[2,256,1792]{2,1,0:T(8,128)}) fusion(bf16[1792,2,128]{2,0,1:T(8,128)(2,1)S(1)} %get-tuple-element.280, pred[256,1792]{1,0:T(8,128)(4,1)S(1)} %iota_compare_fusion.5, bf16[8,256,2,128]{1,3,0,2:T(8,128)(2,1)} %get-tuple-element.279, s32[]{:T(128)S(6)} %copy.69), kind=kOutput, calls=%fused_computation.148.clone.1 | convolution fusion | flops 239470336 | bytes 5638148 | tf_op jit(solution)/shard_map/while/body/eval_jaxpr/sub | solution.py:20
  177.6 3.0 fusion.91
  181.1 4.6 %fusion.90 = (f32[2,256]{1,0:T(2,128)S(1)}, f32[2,256,1792]{2,1,0:T(8,128)}) fusion(bf16[1792,2,128]{2,0,1:T(8,128)(2,1)S(1)} %get-tuple-element.280, pred[256,1792]{1,0:T(8,128)(4,1)S(1)} %iota_compare_fusion.5, bf16[8,256,2,128]{1,3,0,2:T(8,128)(2,1)} %get-tuple-element.279, s32[]{:T(128)S(6)} %copy.69), kind=kOutput, calls=%fused_computation.148.clone.1 | convolution fusion | flops 239470336 | bytes 5638148 | tf_op jit(solution)/shard_map/while/body/eval_jaxpr/sub | solution.py:20
  185.7 3.0 fusion.91
  189.2 4.6 %fusion.90 = (f32[2,256]{1,0:T(2,128)S(1)}, f32[2,256,1792]{2,1,0:T(8,128)}) fusion(bf16[1792,2,128]{2,0,1:T(8,128)(2,1)S(1)} %get-tuple-element.280, pred[256,1792]{1,0:T(8,128)(4,1)S(1)} %iota_compare_fusion.5, bf16[8,256,2,128]{1,3,0,2:T(8,128)(2,1)} %get-tuple-element.279, s32[]{:T(128)S(6)} %copy.69), kind=kOutput, calls=%fused_computation.148.clone.1 | convolution fusion | flops 239470336 | bytes 5638148 | tf_op jit(solution)/shard_map/while/body/eval_jaxpr/sub | solution.py:20
  193.8 3.0 fusion.91
  197.0 25.9 %convolution_convert_fusion = bf16[512,8192]{1,0:T(8,128)(2,1)} fusion(bf16[2048,8192]{1,0:T(8,128)(2,1)} %all-gather.2.cloned.1.call-done, bf16[256,2048]{0,1:T(8,128)(2,1)S(1)} %bitcast.138, bf16[256,2048]{0,1:T(8,128)(2,1)S(1)} %bitcast.139), kind=kOutput, calls=%fused_computation.48 | convolution fusion | flops 17188257792 | bytes 44040192 | tf_op jit(solution)/shard_map/dot_general | solution.py:69
  224.1 143.4 %reduce-scatter.2.cloned.1.call-done = bf16[512,2048]{1,0:T(8,128)(2,1)} async-done(((bf16[512,8192]{1,0:T(8,128)(2,1)}), bf16[512,2048]{1,0:T(8,128)(2,1)}) %reduce-scatter.2.cloned.1.call-update) | async-done | bytes 2097168 | tf_op jit(solution)/shard_map/reduce_scatter | solution.py:77
  367.5 6.5 %gather_fusion.5 = bf16[512,2048]{1,0:T(8,128)(2,1)S(1)} fusion(bf16[512,2048]{1,0:T(8,128)(2,1)} %reduce-scatter.2.cloned.1.call-done, s32[1024]{0:T(1024)S(1)} %pad_clamp_fusion), kind=kCustom, calls=%fused_computation.5 | custom fusion | bytes 4196352 | tf_op jit(solution)/shard_map/jit(_take)/gather | solution.py:45
  386.4 3.5 collective-permute-done.2
  389.9 12.1 %collective-permute-done.4 = bf16[1,64,2048]{2,1,0:T(8,128)(2,1)S(1)} collective-permute-done((bf16[1,64,2048]{2,1,0:T(8,128)(2,1)S(1)}, bf16[1,64,2048]{2,1,0:T(8,128)(2,1)S(1)}, u32[]{:S(2)}, u32[]{:S(2)}) %collective-permute-start.4) | collective-permute-done | bytes 262176 | tf_op jit(solution)/shard_map/ppermute | solution.py:57
  402.1 3.8 scatter_custom_fusion.2
  (160 shorter events, 44.2 us)
Async XLA Ops:
  7.2 189.8 %all-gather.2.cloned.1.call-start = ((), (), s32[]{:S(2)}) async-start(), calls=%async_computation.1 | async-start | bytes 37748736 | tf_op jit(solution)/shard_map/all_gather | solution.py:71
  10.1 0.7 copy-start.11
  10.1 2.0 copy-start.10
  10.1 14.0 %copy-start.9 = (s32[2]{0:T(128)S(1)}, s32[2]{0:T(128)}, u32[]{:S(2)}) copy-start(s32[2]{0:T(128)} %param.22) | copy-start | bytes 28
  10.2 357.3 %reduce-scatter.2.cloned.1.call-start = ((), (), s32[]{:S(2)}) async-start(), calls=%async_computation.2 | async-start | bytes 10485760 | tf_op jit(solution)/shard_map/reduce_scatter | solution.py:77
  24.5 3.4 copy-start
  27.9 5.4 %copy-start.7 = (bf16[512,256]{1,0:T(8,128)(2,1)S(1)}, bf16[512,256]{1,0:T(8,128)(2,1)}, u32[]{:S(2)}) copy-start(bf16[512,256]{1,0:T(8,128)(2,1)} %param.16) | copy-start | bytes 786436
  33.2 8.6 %copy-start.2 = (bf16[28,128,256]{2,1,0:T(8,128)(2,1)S(1)}, bf16[28,128,256]{2,1,0:T(8,128)(2,1)}, u32[]{:S(2)}) copy-start(bf16[28,128,256]{2,1,0:T(8,128)(2,1)} %param.19) | copy-start | bytes 5505028
  33.3 8.6 %copy-start.8 = (bf16[512,256]{1,0:T(8,128)(2,1)S(1)}, bf16[512,256]{1,0:T(8,128)(2,1)}, u32[]{:S(2)}) copy-start(bf16[512,256]{1,0:T(8,128)(2,1)} %param.17) | copy-start | bytes 786436
  45.4 6.2 %copy-start.1 = (bf16[3584,256]{1,0:T(8,128)(2,1)}, bf16[3584,256]{1,0:T(8,128)(2,1)S(1)}, u32[]{:S(2)}) copy-start(bf16[3584,256]{1,0:T(8,128)(2,1)S(1)} %scatter_fusion.1) | copy-start | bytes 5505028
  54.3 2.4 copy-start.4
  56.9 1.5 copy-start.5
  60.9 2.4 copy-start.3
  63.6 1.5 copy-start.6
  375.6 3.7 collective-permute-start
  375.8 9.4 %collective-permute-start.1 = (bf16[1,64,2048]{2,1,0:T(8,128)(2,1)}, bf16[1,64,2048]{2,1,0:T(8,128)(2,1)S(1)}, u32[]{:S(2)}, u32[]{:S(2)}) collective-permute-start(bf16[1,64,2048]{2,1,0:T(8,128)(2,1)} %get-tuple-element.140), channel_id=1, source_target_pairs={{0,8},{4,12},{8,0},{12,4},{16,24},{20,28},{24,16},{28,20},{1,9},{5... | collective-permute-start | bytes 786440 | tf_op jit(solution)/shard_map/ppermute | solution.py:57
  377.3 12.6 %collective-permute-start.2 = (bf16[1,64,2048]{2,1,0:T(8,128)(2,1)S(1)}, bf16[1,64,2048]{2,1,0:T(8,128)(2,1)S(1)}, u32[]{:S(2)}, u32[]{:S(2)}) collective-permute-start(bf16[1,64,2048]{2,1,0:T(8,128)(2,1)S(1)} %get-tuple-element.139), channel_id=1, source_target_pairs={{0,12},{4,8},{8,4},{12,0},{16,28},{20,24},{24,20},{28,16},{1,13},{... | collective-permute-start | bytes 786440 | tf_op jit(solution)/shard_map/ppermute | solution.py:57
  377.6 12.2 %collective-permute-start.3 = (bf16[1,64,2048]{2,1,0:T(8,128)(2,1)S(1)}, bf16[1,64,2048]{2,1,0:T(8,128)(2,1)S(1)}, u32[]{:S(2)}, u32[]{:S(2)}) collective-permute-start(bf16[1,64,2048]{2,1,0:T(8,128)(2,1)S(1)} %get-tuple-element.138), channel_id=1, source_target_pairs={{0,16},{4,20},{8,24},{12,28},{16,0},{20,4},{24,8},{28,12},{1,17},{... | collective-permute-start | bytes 786440 | tf_op jit(solution)/shard_map/ppermute | solution.py:57
  379.1 22.9 %collective-permute-start.4 = (bf16[1,64,2048]{2,1,0:T(8,128)(2,1)S(1)}, bf16[1,64,2048]{2,1,0:T(8,128)(2,1)S(1)}, u32[]{:S(2)}, u32[]{:S(2)}) collective-permute-start(bf16[1,64,2048]{2,1,0:T(8,128)(2,1)S(1)} %get-tuple-element.137), channel_id=1, source_target_pairs={{0,20},{4,16},{8,28},{12,24},{16,4},{20,0},{24,12},{28,8},{1,21},{... | collective-permute-start | bytes 786440 | tf_op jit(solution)/shard_map/ppermute | solution.py:57
  379.3 22.7 %collective-permute-start.5 = (bf16[1,64,2048]{2,1,0:T(8,128)(2,1)S(1)}, bf16[1,64,2048]{2,1,0:T(8,128)(2,1)S(1)}, u32[]{:S(2)}, u32[]{:S(2)}) collective-permute-start(bf16[1,64,2048]{2,1,0:T(8,128)(2,1)S(1)} %get-tuple-element.136), channel_id=1, source_target_pairs={{0,24},{4,28},{8,16},{12,20},{16,8},{20,12},{24,0},{28,4},{1,25},{... | collective-permute-start | bytes 786440 | tf_op jit(solution)/shard_map/ppermute | solution.py:57
  385.2 16.9 %collective-permute-start.6 = (bf16[1,64,2048]{2,1,0:T(8,128)(2,1)S(1)}, bf16[1,64,2048]{2,1,0:T(8,128)(2,1)S(1)}, u32[]{:S(2)}, u32[]{:S(2)}) collective-permute-start(bf16[1,64,2048]{2,1,0:T(8,128)(2,1)S(1)} %get-tuple-element.135), channel_id=1, source_target_pairs={{0,28},{4,24},{8,20},{12,16},{16,12},{20,8},{24,4},{28,0},{1,29},{... | collective-permute-start | bytes 786440 | tf_op jit(solution)/shard_map/ppermute | solution.py:57
Sparse Core Ops, SparseCore 0:
  10.3 163.3 all-gather.1
  223.1 144.3 reduce-scatter.1
